TPU v7x, 128 devices: a whole 4x4x4 slice. The times are simulated.
128 devices in a mesh: dp: 8 (over x, core), table: 16 (over z, y).
Axes of the slice: x: 4, y: 4, z: 4, core: 2. Of those that a mesh axis runs over, the one named last changes fastest.
Arguments:
- user_table: bfloat16 [524288, 256], P(('dp', 'table')), may hold values from -6 to 6
- item_table: bfloat16 [524288, 256], P(('dp', 'table')), may hold values from -6 to 6
- hist_owner: int32 [262144, 1], P(('dp', 'table')), may hold values from 0 to 127; in each aligned block of 2048 rows (0 to 2047, 2048 to 4095, ...) at most 32 rows name the same one
- hist_row: int32 [262144], P(('dp', 'table')), may hold values from 0 to 4095
- hist_seg: int32 [128, 2048], P(('dp', 'table')), may hold values from 0 to 127, never falling along the last dimension, each value on 1 to 64 neighbouring positions
- hist_wix: int32 [262144], P(('dp', 'table')), may hold values from 0 to 63
- bag_weights: bfloat16 [64], replicated, may hold values from 0.099609375 to 1
- item_owner: int32 [16384, 1], P(('dp', 'table')), may hold values from 0 to 127; in each aligned block of 128 rows (0 to 127, 128 to 255, ...) at most 2 rows name the same one
- item_row: int32 [16384], P(('dp', 'table')), may hold values from 0 to 4095
- user_proj: bfloat16 [256, 256], replicated, may hold values from -0.375 to 0.375
- item_proj: bfloat16 [256, 256], replicated, may hold values from -0.375 to 0.375
- logit_scale: float32 [1], replicated, may hold values from 8 to 600
Outputs:
- user_grad: float32 [524288, 256], P(('dp', 'table'))
- item_grad: float32 [524288, 256], P(('dp', 'table'))
- user_proj_grad: float32 [256, 256], replicated
- item_proj_grad: float32 [256, 256], replicated
Inputs may be any that keep to these rules, and one draw needn't show every extreme that they name: `hist_owner`: among the 2048 history ids of one device, no owner is named more than 32 times; some owner exactly 32 times. `item_owner`: among the 128 samples of one device, no owner is named more than 2 times; some owner exactly 2 times. `hist_seg`: each row numbers 128 samples in order; each sample has 1 to 64 ids, one has exactly 64.
All inputs are finite; a program needn't handle non-finite values.
Results may differ from a plain program's by a relative error of at most 0.01.
The roundings to bfloat16 on the way count: a program that leaves them out, or rounds other values in their place, can miss the bound.
Values may be sent and summed in bfloat16 or wider, within the bound.
No kernel may reach another device: no remote copies, remote signals or barrier semaphores. Data moves between devices by JAX's collectives and lax.ppermute only.
A program may use at most 128 MiB of HBM per device.

v0:
```python
import jax
import jax.numpy as jnp
from jax import lax
from jax.sharding import PartitionSpec as P

EPS = 1e-06
AXES = ("dp", "table")


def tower(x, weight):
    u = jnp.dot(x, weight, preferred_element_type=jnp.float32)
    r = lax.rsqrt(jnp.sum(u * u, -1, keepdims=True) + EPS)
    return (u * r, r)


def slot_rank(owner, devices):
    onehot = (owner[:, None] == jnp.arange(devices, dtype=jnp.int32)[None, :]).astype(jnp.int32)
    before = jnp.cumsum(onehot, 0) - onehot
    return jnp.sum(before * onehot, 1)


def pick_rows(table, wanted):
    rows_dev = table.shape[0]
    flat = wanted.reshape(-1)
    onehot = (flat[:, None] == jnp.arange(rows_dev, dtype=jnp.int32)[None, :]).astype(table.dtype)
    picked = jnp.dot(onehot, table, preferred_element_type=jnp.float32).astype(table.dtype)
    return picked.reshape(wanted.shape + table.shape[1:])


def add_rows(rows_dev, wanted, values):
    flat = wanted.reshape(-1)
    onehot = (jnp.arange(rows_dev, dtype=jnp.int32)[:, None] == flat[None, :]).astype(values.dtype)
    return jnp.dot(onehot, values.reshape(flat.shape[0], -1), preferred_element_type=jnp.float32)


def exchange(x):
    return lax.all_to_all(x, AXES, split_axis=1, concat_axis=1, tiled=True)


def local(
    user_table,
    item_table,
    hist_owner,
    hist_row,
    hist_seg,
    hist_wix,
    bag_weights,
    item_owner,
    item_row,
    user_proj,
    item_proj,
    logit_scale,
):
    rows_dev, width = user_table.shape
    n_dp = lax.axis_size("dp")
    n_tab = lax.axis_size("table")
    devices = n_dp * n_tab
    tokens = hist_row.shape[0]
    samples = item_row.shape[0]
    cap = max(2, 2 * tokens // devices)
    cap_item = max(2, 2 * samples // devices)
    slots = cap + cap_item
    myself = lax.axis_index(AXES)
    entries = bag_weights.shape[0]
    segment = hist_seg[0]
    sample_ids = jnp.arange(samples, dtype=jnp.int32)
    owner = jnp.concatenate([hist_owner[:, 0], item_owner[:, 0]])
    rank = jnp.concatenate(
        [slot_rank(hist_owner[:, 0], devices), cap + slot_rank(item_owner[:, 0], devices)]
    )
    row = jnp.concatenate([hist_row, item_row])
    fields = jnp.stack(
        [
            row & 255,
            row >> 8,
            jnp.concatenate([segment, sample_ids]),
            jnp.concatenate([hist_wix, jnp.zeros((samples,), jnp.int32)]),
            jnp.ones_like(row),
        ]
    )
    by_owner = (owner[None, :] == jnp.arange(devices, dtype=jnp.int32)[:, None]).astype(
        jnp.bfloat16
    )
    planes = (fields.astype(jnp.bfloat16)[:, None, :] * by_owner[None, :, :]).reshape(
        -1, owner.shape[0]
    )
    by_rank = (rank[:, None] == jnp.arange(slots, dtype=jnp.int32)[None, :]).astype(jnp.bfloat16)
    table = jnp.dot(planes, by_rank, preferred_element_type=jnp.float32)
    table = table.astype(jnp.int32).reshape(fields.shape[0], devices, slots)
    table = jnp.transpose(table, (0, 2, 1)).reshape(fields.shape[0], slots * devices)
    slot_row = table[0] + 256 * table[1]
    slot_seg = table[2]
    slot_wix = table[3]
    filled = table[4] > 0
    req = jnp.where(filled, slot_row, rows_dev).reshape(slots, devices)
    is_user = jnp.arange(slots * devices, dtype=jnp.int32) < cap * devices
    want = exchange(req)
    user_want = want[:cap]
    goods_want = want[cap:]
    goods_back = exchange(pick_rows(item_table, goods_want))
    user_back = exchange(pick_rows(user_table, user_want))
    wts = jnp.sum(
        jnp.where(
            slot_wix[:, None] == jnp.arange(entries, dtype=jnp.int32)[None, :],
            bag_weights[None, :].astype(jnp.float32),
            0.0,
        ),
        1,
    ).astype(jnp.bfloat16)
    of_sample = filled[None, :] & (slot_seg[None, :] == sample_ids[:, None])
    item_pick = of_sample[:, cap * devices :].astype(jnp.bfloat16)
    item_emb = jnp.dot(
        item_pick, goods_back.reshape(-1, width), preferred_element_type=jnp.float32
    ).astype(jnp.bfloat16)
    vn, rv = tower(item_emb, item_proj)
    vh = vn.astype(jnp.bfloat16)
    vh_all = lax.all_gather(vh, AXES, axis=0, tiled=True)
    coef = jnp.where(
        of_sample[:, : cap * devices], wts[None, : cap * devices], jnp.zeros((), jnp.bfloat16)
    )
    numer = jnp.dot(coef, user_back.reshape(-1, width), preferred_element_type=jnp.float32)
    denom = jnp.sum(coef.astype(jnp.float32), 1)
    bag = (numer / denom[:, None]).astype(jnp.bfloat16)
    un, ru = tower(bag, user_proj)
    uh = un.astype(jnp.bfloat16)
    uh_all = lax.all_gather(uh, AXES, axis=0, tiled=True)
    scale = logit_scale[0]
    total = vh_all.shape[0]
    mine = myself * samples + sample_ids
    everyone = jnp.arange(total, dtype=jnp.int32)
    scores = scale * jnp.dot(uh, vh_all.T, preferred_element_type=jnp.float32)
    top = jnp.max(scores, -1)
    expo = jnp.exp(scores - top[:, None])
    norm = jnp.sum(expo, -1)
    prob = expo / norm[:, None]
    hot = (everyone[None, :] == mine[:, None]).astype(jnp.float32)
    pw = (prob - hot).astype(jnp.bfloat16)
    d_un = scale / total * jnp.dot(pw, vh_all, preferred_element_type=jnp.float32)
    d_u = ru * (d_un - un * jnp.sum(un * d_un, -1, keepdims=True))
    highest = lax.Precision.HIGHEST
    user_part = jnp.dot(bag.astype(jnp.float32).T, d_u, precision=highest)
    d_bag = jnp.dot(d_u, user_proj.astype(jnp.float32).T, precision=highest)
    n_user = cap * devices
    pick = jnp.concatenate([d_bag, denom[:, None]], axis=1)
    per_slot = jnp.dot(of_sample[:, :n_user].T.astype(jnp.float32), pick, precision=highest)
    g_slot = (wts[:n_user].astype(jnp.float32) / per_slot[:, width])[:, None] * per_slot[:, :width]
    g_slot = jnp.where(filled[:n_user, None], g_slot, 0.0)
    got_user = exchange(g_slot.astype(jnp.bfloat16).reshape(cap, devices, width))
    user_grad = add_rows(rows_dev, user_want, got_user)
    stats = jnp.concatenate([top, norm]).reshape(1, 1, -1)
    stats = jnp.broadcast_to(stats, (devices, 1, stats.shape[-1]))
    stats = jnp.pad(stats, ((0, 0), (0, 0), (0, -stats.shape[-1] % width)))
    stats = stats.reshape(devices, -1, width)
    user_parts = jnp.transpose(user_part.reshape(-1, devices, width), (1, 0, 2))
    n_stat = stats.shape[1]
    got_s = lax.all_to_all(
        jnp.concatenate([stats, user_parts], axis=1), AXES, split_axis=0, concat_axis=0, tiled=True
    )
    flat_stats = got_s[:, :n_stat].reshape(devices, -1)
    top_all = flat_stats[:, :samples].reshape(total)
    norm_all = flat_stats[:, samples : 2 * samples].reshape(total)
    user_red = jnp.sum(got_s[:, n_stat:], 0)
    scores_c = scale * jnp.dot(vh, uh_all.T, preferred_element_type=jnp.float32)
    prob_c = jnp.exp(scores_c - top_all[None, :]) * (1.0 / norm_all)[None, :]
    hot_c = (everyone[None, :] == mine[:, None]).astype(jnp.float32)
    pw_c = (prob_c - hot_c).astype(jnp.bfloat16)
    d_vn = scale / total * jnp.dot(pw_c, uh_all, preferred_element_type=jnp.float32)
    d_v = rv * (d_vn - vn * jnp.sum(vn * d_vn, -1, keepdims=True))
    goods_part = jnp.dot(item_emb.astype(jnp.float32).T, d_v, precision=highest)
    d_v_slot = jnp.dot(item_pick.T.astype(jnp.float32), d_v, precision=highest)
    goods_parts = goods_part.reshape(-1, devices, width)
    chunk = goods_parts.shape[0]
    hi = goods_parts.astype(jnp.bfloat16)
    lo = (goods_parts - hi.astype(jnp.float32)).astype(jnp.bfloat16)
    send = jnp.concatenate(
        [d_v_slot.astype(jnp.bfloat16).reshape(cap_item, devices, width), hi, lo], axis=0
    )
    got = exchange(send)
    tail = got[cap_item:].astype(jnp.float32)
    goods_red = jnp.sum(tail[:chunk] + tail[chunk:], 1)
    red = jnp.concatenate([user_red, goods_red])
    spread = exchange(jnp.broadcast_to(red[:, None], (red.shape[0], devices, width)))
    user_proj_grad = spread[:chunk].reshape(width, width)
    item_proj_grad = spread[chunk:].reshape(width, width)
    item_grad = add_rows(rows_dev, goods_want, got[:cap_item])
    return (user_grad, item_grad, user_proj_grad, item_proj_grad)


def solution(mesh):
    in_specs = (
        P(AXES, None),
        P(AXES, None),
        P(AXES, None),
        P(AXES),
        P(AXES, None),
        P(AXES),
        P(),
        P(AXES, None),
        P(AXES),
        P(),
        P(),
        P(),
    )
    out_specs = (P(AXES, None), P(AXES, None), P(), P())
    return jax.shard_map(local, mesh=mesh, in_specs=in_specs, out_specs=out_specs, check_vma=False)
```

profile of v0, /device:TPU:1, one launch (start us, length us, event | category | flops | bytes accessed | tf_op | source)
XLA Modules:
  0.0 283.7 jit_solution(170055418482812964)
XLA Ops:
  18.5 11.5 %all-to-all-start = ((s32[34,128,1]{0,2,1:T(1,128)}), s32[34,128,1]{0,2,1:T(1,128)S(1)}, u32[]{:S(2)}, u32[]{:S(2)}) async-start(s32[34,128,1]{0,2,1:T(1,128)} %copy.72), calls=%async_computation | async-start | bytes 131072 | tf_op jit(solution)/shard_map/all_to_all | solution.py:37
  30.0 9.7 %all-to-all-done = s32[34,128,1]{0,2,1:T(1,128)S(1)} async-done(((s32[34,128,1]{0,2,1:T(1,128)}), s32[34,128,1]{0,2,1:T(1,128)S(1)}, u32[]{:S(2)}, u32[]{:S(2)}) %all-to-all-start) | async-done | bytes 17440 | tf_op jit(solution)/shard_map/all_to_all | solution.py:37
  43.1 4.3 %all-to-all-start.2 = ((bf16[2,128,256]{2,0,1:T(2,128)(2,1)}), bf16[2,128,256]{2,0,1:T(2,128)(2,1)S(1)}, u32[]{:S(2)}, u32[]{:S(2)}) async-start(bf16[2,128,256]{2,0,1:T(2,128)(2,1)} %copy.77), calls=%async_computation.2 | async-start | bytes 262144 | tf_op jit(solution)/shard_map/all_to_all | solution.py:37
  48.1 9.5 %all-to-all-done.2 = bf16[2,128,256]{2,0,1:T(2,128)(2,1)S(1)} async-done(((bf16[2,128,256]{2,0,1:T(2,128)(2,1)}), bf16[2,128,256]{2,0,1:T(2,128)(2,1)S(1)}, u32[]{:S(2)}, u32[]{:S(2)}) %all-to-all-start.2) | async-done | bytes 131104 | tf_op jit(solution)/shard_map/all_to_all | solution.py:37
  58.9 12.3 %fusion.11 = bf16[4096,256]{1,0:T(8,128)(2,1)S(1)} fusion(bf16[4096,256]{1,0:T(8,128)(2,1)S(1)} %copy-done, s32[4096]{0:T(1024)S(1)} %bitcast.105), kind=kOutput, calls=%fused_computation.18 | convolution fusion | flops 8607760384 | bytes 4210688 | tf_op jit(solution)/shard_map/dot_general | solution.py:26
  71.2 2.5 copy.74
  73.7 4.0 %all-to-all-start.1 = ((bf16[32,128,256]{2,0,1:T(8,128)(2,1)}), bf16[32,128,256]{2,0,1:T(8,128)(2,1)S(1)}, u32[]{:S(2)}, u32[]{:S(2)}) async-start(bf16[32,128,256]{2,0,1:T(8,128)(2,1)} %copy.74), calls=%async_computation.1 | async-start | bytes 4194304 | tf_op jit(solution)/shard_map/all_to_all | solution.py:37
  79.1 30.2 %all-to-all-done.1 = bf16[32,128,256]{2,0,1:T(8,128)(2,1)S(1)} async-done(((bf16[32,128,256]{2,0,1:T(8,128)(2,1)}), bf16[32,128,256]{2,0,1:T(8,128)(2,1)S(1)}, u32[]{:S(2)}, u32[]{:S(2)}) %all-to-all-start.1) | async-done | bytes 2097184 | tf_op jit(solution)/shard_map/all_to_all | solution.py:37
  113.1 22.4 %all-gather.3.cloned.1.call-done = bf16[16384,256]{1,0:T(8,128)(2,1)} async-done(((bf16[128,256]{1,0:T(8,128)(2,1)}), bf16[16384,256]{1,0:T(8,128)(2,1)}) %all-gather.3.cloned.1.call-update) | async-done | bytes 8388624 | tf_op jit(solution)/shard_map/all_gather | solution.py:117
  135.5 6.3 %fusion.57 = (f32[128]{0:T(128)S(1)}, f32[128,16384]{1,0:T(8,128)S(1)}) fusion(bf16[128,256]{1,0:T(8,128)(2,1)} %multiply_convert_fusion.1, bf16[16384,256]{1,0:T(8,128)(2,1)} %all-gather.3.cloned.1.call-done, f32[]{:T(128)} %bitcast.78), kind=kOutput, calls=%fused_computation.123 | convolution fusion | flops 1077936000 | bytes 16843268 | tf_op jit(solution)/shard_map/dot_general | solution.py:131
  145.2 2.9 %multiply_reduce_fusion.1 = (f32[128]{0:T(128)S(1)}, f32[128,256]{1,0:T(8,128)S(1)}) fusion(f32[128,256]{1,0:T(8,128)S(1)} %get-tuple-element.19, f32[128]{0:T(128)S(1)} %add_rsqrt_fusion.1, bf16[16384,256]{1,0:T(8,128)(2,1)S(1)} %copy-done.3, f32[128,16384]{1,0:T(8,128)S(1)} %get-tuple-element.21, s32[128]{0:T(128)S(1)} %iota_add_fusion, ...), kind=kOutput, calls=%fused_computation.79 | convolution fusion | flops 1086455680 | bytes 17041924 | tf_op jit(solution)/shard_map/dot_general | solution.py:138
  154.2 5.4 %all-to-all-start.4 = ((f32[128,3,256]{2,1,0:T(4,128)}), f32[128,3,256]{2,1,0:T(4,128)S(1)}, u32[]{:S(2)}, u32[]{:S(2)}) async-start(f32[128,3,256]{2,1,0:T(4,128)} %pad_maximum_fusion), calls=%async_computation.4 | async-start | bytes 1048576 | tf_op jit(solution)/shard_map/all_to_all | solution.py:156
  159.6 2.8 fusion.19
  162.9 3.4 %copy.80 = bf16[32,128,256]{2,0,1:T(8,128)(2,1)} copy(bf16[32,128,256]{1,0,2:T(8,128)(2,1)S(1)} %bitcast.81) | data formatting | bytes 4194304 | tf_op jit(solution)/shard_map/reshape | solution.py:148
  166.3 7.3 %all-to-all-done.4 = f32[128,3,256]{2,1,0:T(4,128)S(1)} async-done(((f32[128,3,256]{2,1,0:T(4,128)}), f32[128,3,256]{2,1,0:T(4,128)S(1)}, u32[]{:S(2)}, u32[]{:S(2)}) %all-to-all-start.4) | async-done | bytes 393248 | tf_op jit(solution)/shard_map/all_to_all | solution.py:156
  173.6 4.0 %all-to-all-start.3 = ((bf16[32,128,256]{2,0,1:T(8,128)(2,1)}), bf16[32,128,256]{2,0,1:T(8,128)(2,1)S(1)}, u32[]{:S(2)}, u32[]{:S(2)}) async-start(bf16[32,128,256]{2,0,1:T(8,128)(2,1)} %copy.80), calls=%async_computation.3 | async-start | bytes 4194304 | tf_op jit(solution)/shard_map/all_to_all | solution.py:37
  178.4 40.6 %all-gather.5.cloned.1.call-done = bf16[16384,256]{1,0:T(8,128)(2,1)} async-done(((bf16[128,256]{1,0:T(8,128)(2,1)}), bf16[16384,256]{1,0:T(8,128)(2,1)}) %all-gather.5.cloned.1.call-update) | async-done | bytes 8388624 | tf_op jit(solution)/shard_map/all_gather | solution.py:126
  219.0 9.9 %multiply_reduce_fusion = (f32[128]{0:T(128)S(1)}, f32[128,256]{1,0:T(8,128)S(1)}) fusion(f32[128,256]{1,0:T(8,128)S(1)} %get-tuple-element.17, f32[128]{0:T(128)S(1)} %add_rsqrt_fusion, bf16[16384,256]{1,0:T(8,128)(2,1)} %all-gather.5.cloned.1.call-done, bf16[128,256]{1,0:T(8,128)(2,1)} %multiply_convert_fusion, f32[16384]{0:T(1024)} %get-tuple-element.13, ...), kind=kOutput, calls=%fused_computation.77 | convolution fusion | flops 2162294784 | bytes 8848904 | tf_op jit(solution)/shard_map/dot_general | solution.py:167
  231.5 6.0 %all-to-all-start.5 = ((bf16[6,128,256]{2,0,1:T(8,128)(2,1)}), bf16[6,128,256]{2,0,1:T(8,128)(2,1)S(1)}, u32[]{:S(2)}, u32[]{:S(2)}) async-start(bf16[6,128,256]{2,0,1:T(8,128)(2,1)} %pad_maximum_fusion.1), calls=%async_computation.5 | async-start | bytes 1048576 | tf_op jit(solution)/shard_map/all_to_all | solution.py:37
  238.7 2.5 copy.81
  241.2 10.3 %all-to-all-done.5 = bf16[6,128,256]{2,0,1:T(8,128)(2,1)S(1)} async-done(((bf16[6,128,256]{2,0,1:T(8,128)(2,1)}), bf16[6,128,256]{2,0,1:T(8,128)(2,1)S(1)}, u32[]{:S(2)}, u32[]{:S(2)}) %all-to-all-start.5) | async-done | bytes 393248 | tf_op jit(solution)/shard_map/all_to_all | solution.py:37
  252.8 4.3 %all-to-all-start.6 = ((f32[4,128,256]{2,0,1:T(4,128)}), f32[4,128,256]{2,0,1:T(4,128)S(1)}, u32[]{:S(2)}, u32[]{:S(2)}) async-start(f32[4,128,256]{2,0,1:T(4,128)} %broadcast_in_dim.55), calls=%async_computation.6 | async-start | bytes 1048576 | tf_op jit(solution)/shard_map/all_to_all | solution.py:37
  257.1 14.9 %fusion = f32[4096,256]{1,0:T(8,128)} fusion(bf16[4096,256]{1,0:T(8,128)(2,1)} %bitcast.84, s32[4096]{0:T(1024)S(1)} %bitcast.106), kind=kOutput, calls=%fused_computation.2 | convolution fusion | flops 8606711808 | bytes 6307840 | tf_op jit(solution)/shard_map/dot_general | solution.py:33
  272.1 2.8 fusion.17
  (114 shorter events, 38.2 us)
Async XLA Ops:
  7.2 51.8 %copy-start = (bf16[4096,256]{1,0:T(8,128)(2,1)S(1)}, bf16[4096,256]{1,0:T(8,128)(2,1)}, u32[]{:S(2)}) copy-start(bf16[4096,256]{1,0:T(8,128)(2,1)} %param.12) | copy-start | bytes 6291460
  7.2 8.0 %copy-start.8 = (s32[2048,1]{0,1:T(1,128)S(1)}, s32[2048,1]{0,1:T(1,128)}, u32[]{:S(2)}) copy-start(s32[2048,1]{0,1:T(1,128)} %param.14) | copy-start | bytes 24580
  7.2 8.7 %copy-start.10 = (s32[128]{0:T(128)S(1)}, s32[128]{0:T(128)}, u32[]{:S(2)}) copy-start(s32[128]{0:T(128)} %param.20) | copy-start | bytes 1540
  7.2 8.7 %copy-start.9 = (s32[2048]{0:T(1024)S(1)}, s32[2048]{0:T(1024)}, u32[]{:S(2)}) copy-start(s32[2048]{0:T(1024)} %param.15) | copy-start | bytes 24580
  12.6 1.0 copy-start.4
  16.3 41.5 %copy-start.7 = (bf16[256,256]{1,0:T(8,128)(2,1)S(1)}, bf16[256,256]{1,0:T(8,128)(2,1)}, u32[]{:S(2)}) copy-start(bf16[256,256]{1,0:T(8,128)(2,1)} %param.22) | copy-start | bytes 393220
  18.5 21.2 %all-to-all-start = ((s32[34,128,1]{0,2,1:T(1,128)}), s32[34,128,1]{0,2,1:T(1,128)S(1)}, u32[]{:S(2)}, u32[]{:S(2)}) async-start(s32[34,128,1]{0,2,1:T(1,128)} %copy.72), calls=%async_computation | async-start | bytes 131072 | tf_op jit(solution)/shard_map/all_to_all | solution.py:37
  43.1 14.5 %all-to-all-start.2 = ((bf16[2,128,256]{2,0,1:T(2,128)(2,1)}), bf16[2,128,256]{2,0,1:T(2,128)(2,1)S(1)}, u32[]{:S(2)}, u32[]{:S(2)}) async-start(bf16[2,128,256]{2,0,1:T(2,128)(2,1)} %copy.77), calls=%async_computation.2 | async-start | bytes 262144 | tf_op jit(solution)/shard_map/all_to_all | solution.py:37
  47.4 88.1 %all-gather.3.cloned.1.call-start = ((), (), s32[]{:S(2)}) async-start(), calls=%async_computation.7 | async-start | bytes 8454144 | tf_op jit(solution)/shard_map/all_gather | solution.py:117
  71.2 7.1 %copy-start.11 = (bf16[64]{0:T(256)(128)(2,1)S(1)}, bf16[64]{0:T(256)(128)(2,1)}, u32[]{:S(2)}) copy-start(bf16[64]{0:T(256)(128)(2,1)} %param.18) | copy-start | bytes 388
  73.7 35.6 %all-to-all-start.1 = ((bf16[32,128,256]{2,0,1:T(8,128)(2,1)}), bf16[32,128,256]{2,0,1:T(8,128)(2,1)S(1)}, u32[]{:S(2)}, u32[]{:S(2)}) async-start(bf16[32,128,256]{2,0,1:T(8,128)(2,1)} %copy.74), calls=%async_computation.1 | async-start | bytes 4194304 | tf_op jit(solution)/shard_map/all_to_all | solution.py:37
  77.7 141.3 %all-gather.5.cloned.1.call-start = ((), (), s32[]{:S(2)}) async-start(), calls=%async_computation.8 | async-start | bytes 8454144 | tf_op jit(solution)/shard_map/all_gather | solution.py:126
  79.1 32.1 %copy-start.6 = (bf16[256,256]{1,0:T(8,128)(2,1)S(1)}, bf16[256,256]{1,0:T(8,128)(2,1)}, u32[]{:S(2)}) copy-start(bf16[256,256]{1,0:T(8,128)(2,1)} %param.21) | copy-start | bytes 393220
  141.8 3.4 %copy-start.3 = (bf16[16384,256]{1,0:T(8,128)(2,1)S(1)}, bf16[16384,256]{1,0:T(8,128)(2,1)}, u32[]{:S(2)}) copy-start(bf16[16384,256]{1,0:T(8,128)(2,1)} %all-gather.3.cloned.1.call-done) | copy-start | bytes 25165828
  150.4 2.0 copy-start.2
  154.2 19.4 %all-to-all-start.4 = ((f32[128,3,256]{2,1,0:T(4,128)}), f32[128,3,256]{2,1,0:T(4,128)S(1)}, u32[]{:S(2)}, u32[]{:S(2)}) async-start(f32[128,3,256]{2,1,0:T(4,128)} %pad_maximum_fusion), calls=%async_computation.4 | async-start | bytes 1048576 | tf_op jit(solution)/shard_map/all_to_all | solution.py:156
  173.6 55.3 %copy-start.5 = (f32[128,3,256]{2,1,0:T(4,128)}, f32[128,3,256]{2,1,0:T(4,128)S(1)}, u32[]{:S(2)}) copy-start(f32[128,3,256]{2,1,0:T(4,128)S(1)} %all-to-all-done.4) | copy-start | bytes 1179652
  173.6 57.9 %all-to-all-start.3 = ((bf16[32,128,256]{2,0,1:T(8,128)(2,1)}), bf16[32,128,256]{2,0,1:T(8,128)(2,1)S(1)}, u32[]{:S(2)}, u32[]{:S(2)}) async-start(bf16[32,128,256]{2,0,1:T(8,128)(2,1)} %copy.80), calls=%async_computation.3 | async-start | bytes 4194304 | tf_op jit(solution)/shard_map/all_to_all | solution.py:37
  231.5 20.1 %all-to-all-start.5 = ((bf16[6,128,256]{2,0,1:T(8,128)(2,1)}), bf16[6,128,256]{2,0,1:T(8,128)(2,1)S(1)}, u32[]{:S(2)}, u32[]{:S(2)}) async-start(bf16[6,128,256]{2,0,1:T(8,128)(2,1)} %pad_maximum_fusion.1), calls=%async_computation.5 | async-start | bytes 1048576 | tf_op jit(solution)/shard_map/all_to_all | solution.py:37
  252.8 22.1 %all-to-all-start.6 = ((f32[4,128,256]{2,0,1:T(4,128)}), f32[4,128,256]{2,0,1:T(4,128)S(1)}, u32[]{:S(2)}, u32[]{:S(2)}) async-start(f32[4,128,256]{2,0,1:T(4,128)} %broadcast_in_dim.55), calls=%async_computation.6 | async-start | bytes 1048576 | tf_op jit(solution)/shard_map/all_to_all | solution.py:37
  272.1 4.5 %copy-start.1 = (bf16[4096,256]{1,0:T(8,128)(2,1)S(1)}, bf16[4096,256]{1,0:T(8,128)(2,1)}, u32[]{:S(2)}) copy-start(bf16[4096,256]{1,0:T(8,128)(2,1)} %param.12) | copy-start | bytes 6291460
Sparse Core Ops, SparseCore 0:
  59.0 76.4 all-gather.2
  139.2 79.7 all-gather.4
where the time goes:
time: 289 us; the launch traced here: 284 us
  waiting for transfers between devices  130 us (45%)
  matrix products  57.4 us (20%)
  starting transfers between devices  40.4 us (14%)
  local copies, waits for them, and re-layouts  21.6 us (7%)
  other arithmetic  18.7 us (6%)
  between operations  15.5 us (5%)
    all_to_all x6, waiting for transfers between devices, exchange(): return lax.all_to_all(x, AXES, split_axis=1, concat_axis=1, tiled=True)  59.7 us
    all_gather x1, waiting for transfers between devices, local(): uh_all = lax.all_gather(uh, AXES, axis=0, tiled=True)  40.6 us
    all_to_all x6, starting transfers between devices, exchange(): return lax.all_to_all(x, AXES, split_axis=1, concat_axis=1, tiled=True)  34.1 us
    all_gather x1, waiting for transfers between devices, local(): vh_all = lax.all_gather(vh, AXES, axis=0, tiled=True)  22.4 us
    dot_general x2, matrix products, add_rows(): jnp.dot(onehot, values.reshape(flat.shape[0], -1), preferred_element_type...  17.7 us
    dot_general x2, matrix products, pick_rows(): jnp.dot(onehot, table, preferred_element_type=jnp.float32)  14.7 us
    dot_general x1, matrix products, local(): jnp.dot(pw_c, uh_all, preferred_element_type=jnp.float32)  9.92 us
    all_to_all x1, waiting for transfers between devices, local(): lax.all_to_all(jnp.concatenate([stats, user_parts], axis=1), AXES, split_...  7.28 us
  transfers between devices with their start and end apart: 9, of which 7 were waited for; matrix products, arithmetic and copies ran while one was open for 27% of the time, Pallas kernels for 0%

commit v1 on v0

--- a/solution.py
+++ b/solution.py
@@ -123,7 +123,9 @@
     bag = (numer / denom[:, None]).astype(jnp.bfloat16)
     un, ru = tower(bag, user_proj)
     uh = un.astype(jnp.bfloat16)
-    uh_all = lax.all_gather(uh, AXES, axis=0, tiled=True)
+    uh_all = jnp.concatenate(
+        lax.all_to_all(jnp.stack([uh] * lax.axis_size(AXES)), AXES, 0, 0), axis=0
+    )
     scale = logit_scale[0]
     total = vh_all.shape[0]
     mine = myself * samples + sample_ids

time: 289 us -> 392 us (1.36)
  waiting for transfers between devices: 130 us -> 216 us
  blocking collectives: 0 us -> 19.2 us
  other arithmetic: 18.7 us -> 12.3 us
  starting transfers between devices: 40.4 us -> 44.7 us
    all_to_all x1, waiting for transfers between devices: 7.28 us -> 101 us  [local(): lax.all_to_all(jnp.stack([uh] * lax.axis_size(AXES)), AXES, 0, 0)]
    all_gather x1 -> x0, waiting for transfers between devices: 40.6 us -> none  [local(): uh_all = lax.all_gather(uh, AXES, axis=0, tiled=True)]
    all_to_all x6, waiting for transfers between devices: 59.7 us -> 91.2 us  [exchange(): return lax.all_to_all(x, AXES, split_axis=1, concat_axis=1, tiled=True)]
    all_to_all x0 -> x1, blocking collectives: none -> 19.2 us  [local(): lax.all_to_all(jnp.concatenate([stats, user_parts], axis=1), AXES, split_...]
    all_to_all x6, starting transfers between devices: 34.1 us -> 38.6 us  [exchange(): return lax.all_to_all(x, AXES, split_axis=1, concat_axis=1, tiled=True)]
    another operation x3 -> x4, local copies, waits for them, and re-layouts: 0.35 us -> 4.6 us  [the longest x1 4.25 us: local(): jnp.stack([uh] * lax.axis_size(AXES))]
  transfers between devices with their start and end apart: 9 -> 8, of which waited for: 7 -> 8; matrix products, arithmetic and copies ran while one was open for 27% -> 8% of each run, Pallas kernels for 0% -> 0%
where the time goes in v1:
time: 392 us; the launch traced here: 387 us
  waiting for transfers between devices  216 us (55%)
  matrix products  55.7 us (14%)
  starting transfers between devices  44.7 us (11%)
  local copies, waits for them, and re-layouts  23.5 us (6%)
  blocking collectives  19.2 us (5%)
  between operations  15.6 us (4%)
  other arithmetic  12.3 us (3%)
    all_to_all x1, waiting for transfers between devices, local(): lax.all_to_all(jnp.stack([uh] * lax.axis_size(AXES)), AXES, 0, 0)  101 us
    all_to_all x6, waiting for transfers between devices, exchange(): return lax.all_to_all(x, AXES, split_axis=1, concat_axis=1, tiled=True)  91.2 us
    all_to_all x6, starting transfers between devices, exchange(): return lax.all_to_all(x, AXES, split_axis=1, concat_axis=1, tiled=True)  38.6 us
    all_gather x1, waiting for transfers between devices, local(): vh_all = lax.all_gather(vh, AXES, axis=0, tiled=True)  24 us
    all_to_all x1, blocking collectives, local(): lax.all_to_all(jnp.concatenate([stats, user_parts], axis=1), AXES, split_...  19.2 us
    dot_general x2, matrix products, add_rows(): jnp.dot(onehot, values.reshape(flat.shape[0], -1), preferred_element_type...  16 us
    dot_general x2, matrix products, pick_rows(): jnp.dot(onehot, table, preferred_element_type=jnp.float32)  14.6 us
    dot_general x1, matrix products, local(): jnp.dot(pw_c, uh_all, preferred_element_type=jnp.float32)  9.88 us
  transfers between devices with their start and end apart: 8, of which 8 were waited for; matrix products, arithmetic and copies ran while one was open for 8% of the time, Pallas kernels for 0%

profile of v1, /device:TPU:1, one launch (start us, length us, event | category | flops | bytes accessed | tf_op | source)
XLA Modules:
  0.0 386.9 jit_solution(11842535581947616337)
XLA Ops:
  14.3 11.5 %all-to-all-start = ((s32[34,128,1]{0,2,1:T(1,128)}), s32[34,128,1]{0,2,1:T(1,128)S(1)}, u32[]{:S(2)}, u32[]{:S(2)}) async-start(s32[34,128,1]{0,2,1:T(1,128)} %copy.72), calls=%async_computation | async-start | bytes 131072 | tf_op jit(solution)/shard_map/all_to_all | solution.py:37
  25.8 9.7 %all-to-all-done = s32[34,128,1]{0,2,1:T(1,128)S(1)} async-done(((s32[34,128,1]{0,2,1:T(1,128)}), s32[34,128,1]{0,2,1:T(1,128)S(1)}, u32[]{:S(2)}, u32[]{:S(2)}) %all-to-all-start) | async-done | bytes 17440 | tf_op jit(solution)/shard_map/all_to_all | solution.py:37
  38.9 4.3 %all-to-all-start.2 = ((bf16[2,128,256]{2,0,1:T(2,128)(2,1)}), bf16[2,128,256]{2,0,1:T(2,128)(2,1)S(1)}, u32[]{:S(2)}, u32[]{:S(2)}) async-start(bf16[2,128,256]{2,0,1:T(2,128)(2,1)} %copy.77), calls=%async_computation.2 | async-start | bytes 262144 | tf_op jit(solution)/shard_map/all_to_all | solution.py:37
  43.9 9.5 %all-to-all-done.2 = bf16[2,128,256]{2,0,1:T(2,128)(2,1)S(1)} async-done(((bf16[2,128,256]{2,0,1:T(2,128)(2,1)}), bf16[2,128,256]{2,0,1:T(2,128)(2,1)S(1)}, u32[]{:S(2)}, u32[]{:S(2)}) %all-to-all-start.2) | async-done | bytes 131104 | tf_op jit(solution)/shard_map/all_to_all | solution.py:37
  54.7 12.3 %fusion.11 = bf16[4096,256]{1,0:T(8,128)(2,1)S(1)} fusion(bf16[4096,256]{1,0:T(8,128)(2,1)S(1)} %copy-done, s32[4096]{0:T(1024)S(1)} %bitcast.106), kind=kOutput, calls=%fused_computation.18 | convolution fusion | flops 8607760384 | bytes 4210688 | tf_op jit(solution)/shard_map/dot_general | solution.py:26
  69.5 4.6 %all-to-all-start.1 = ((bf16[32,128,256]{2,0,1:T(8,128)(2,1)}), bf16[32,128,256]{2,0,1:T(8,128)(2,1)S(1)}, u32[]{:S(2)}, u32[]{:S(2)}) async-start(bf16[32,128,256]{2,0,1:T(8,128)(2,1)} %copy.74), calls=%async_computation.1 | async-start | bytes 4194304 | tf_op jit(solution)/shard_map/all_to_all | solution.py:37
  75.7 30.0 %all-to-all-done.1 = bf16[32,128,256]{2,0,1:T(8,128)(2,1)S(1)} async-done(((bf16[32,128,256]{2,0,1:T(8,128)(2,1)}), bf16[32,128,256]{2,0,1:T(8,128)(2,1)S(1)}, u32[]{:S(2)}, u32[]{:S(2)}) %all-to-all-start.1) | async-done | bytes 2097184 | tf_op jit(solution)/shard_map/all_to_all | solution.py:37
  107.9 24.0 %all-gather.2.cloned.1.call-done = bf16[16384,256]{1,0:T(8,128)(2,1)} async-done(((bf16[128,256]{1,0:T(8,128)(2,1)}), bf16[16384,256]{1,0:T(8,128)(2,1)}) %all-gather.2.cloned.1.call-update) | async-done | bytes 8388624 | tf_op jit(solution)/shard_map/all_gather | solution.py:117
  131.9 6.3 %fusion.57 = (f32[128]{0:T(128)S(1)}, f32[128,16384]{1,0:T(8,128)S(1)}) fusion(bf16[128,256]{1,0:T(8,128)(2,1)S(1)} %multiply_convert_fusion.1, bf16[16384,256]{1,0:T(8,128)(2,1)} %all-gather.2.cloned.1.call-done, f32[]{:T(128)} %bitcast.79), kind=kOutput, calls=%fused_computation.123 | convolution fusion | flops 1077936000 | bytes 16843268 | tf_op jit(solution)/shard_map/dot_general | solution.py:133
  141.6 2.9 multiply_reduce_fusion.1
  145.5 19.2 %all_to_all.41 = f32[128,3,256]{2,1,0:T(4,128)S(1)} all-to-all(f32[128,3,256]{2,1,0:T(4,128)S(1)} %pad_maximum_fusion), channel_id=1, replica_groups=mesh['dp'=8,'table'=16] {'dp','table'}, dimensions={0} | all-to-all | bytes 786432 | tf_op jit(solution)/shard_map/all_to_all | solution.py:158
  164.7 4.3 %stack.11 = bf16[128,128,256]{2,1,0:T(8,128)(2,1)} broadcast(bf16[128,256]{1,0:T(8,128)(2,1)S(1)} %multiply_convert_fusion.1), dimensions={1,2} | broadcast | bytes 8454144 | tf_op jit(solution)/shard_map/stack | solution.py:127
  169.0 5.7 %all-to-all-start.4 = ((bf16[128,128,256]{2,1,0:T(8,128)(2,1)}), bf16[128,128,256]{2,1,0:T(8,128)(2,1)}, u32[]{:S(2)}, u32[]{:S(2)}) async-start(bf16[128,128,256]{2,1,0:T(8,128)(2,1)} %stack.11), calls=%async_computation.4 | async-start | bytes 16777216 | tf_op jit(solution)/shard_map/all_to_all | solution.py:127
  175.3 100.6 %all-to-all-done.4 = bf16[128,128,256]{2,1,0:T(8,128)(2,1)} async-done(((bf16[128,128,256]{2,1,0:T(8,128)(2,1)}), bf16[128,128,256]{2,1,0:T(8,128)(2,1)}, u32[]{:S(2)}, u32[]{:S(2)}) %all-to-all-start.4) | async-done | bytes 8388640 | tf_op jit(solution)/shard_map/all_to_all | solution.py:127
  275.9 9.9 %multiply_reduce_fusion = (f32[128]{0:T(128)S(1)}, f32[128,256]{1,0:T(8,128)S(1)}) fusion(f32[128,256]{1,0:T(8,128)S(1)} %get-tuple-element.17, f32[128]{0:T(128)S(1)} %add_rsqrt_fusion, bf16[16384,256]{1,0:T(8,128)(2,1)} %bitcast.21, bf16[128,256]{1,0:T(8,128)(2,1)S(1)} %copy-done.5, f32[16384]{0:T(1024)S(1)} %get-tuple-element.13, ...), kind=kOutput, calls=%fused_computation.77 | convolution fusion | flops 2162294784 | bytes 8848904 | tf_op jit(solution)/shard_map/dot_general | solution.py:169
  288.3 9.8 %all-to-all-start.6 = ((bf16[6,128,256]{2,0,1:T(8,128)(2,1)}), bf16[6,128,256]{2,0,1:T(8,128)(2,1)S(1)}, u32[]{:S(2)}, u32[]{:S(2)}) async-start(bf16[6,128,256]{2,0,1:T(8,128)(2,1)} %pad_maximum_fusion.1), calls=%async_computation.6 | async-start | bytes 1048576 | tf_op jit(solution)/shard_map/all_to_all | solution.py:37
  302.4 9.9 %all-to-all-done.6 = bf16[6,128,256]{2,0,1:T(8,128)(2,1)S(1)} async-done(((bf16[6,128,256]{2,0,1:T(8,128)(2,1)}), bf16[6,128,256]{2,0,1:T(8,128)(2,1)S(1)}, u32[]{:S(2)}, u32[]{:S(2)}) %all-to-all-start.6) | async-done | bytes 393248 | tf_op jit(solution)/shard_map/all_to_all | solution.py:37
  313.5 4.0 %all-to-all-start.7 = ((f32[4,128,256]{2,0,1:T(4,128)}), f32[4,128,256]{2,0,1:T(4,128)S(1)}, u32[]{:S(2)}, u32[]{:S(2)}) async-start(f32[4,128,256]{2,0,1:T(4,128)} %broadcast_in_dim.55), calls=%async_computation.7 | async-start | bytes 1048576 | tf_op jit(solution)/shard_map/all_to_all | solution.py:37
  317.5 2.8 fusion.19
  320.8 3.4 copy.80
  324.3 7.4 %all-to-all-done.7 = f32[4,128,256]{2,0,1:T(4,128)S(1)} async-done(((f32[4,128,256]{2,0,1:T(4,128)}), f32[4,128,256]{2,0,1:T(4,128)S(1)}, u32[]{:S(2)}, u32[]{:S(2)}) %all-to-all-start.7) | async-done | bytes 524320 | tf_op jit(solution)/shard_map/all_to_all | solution.py:37
  331.7 4.4 %all-to-all-start.3 = ((bf16[32,128,256]{2,0,1:T(8,128)(2,1)}), bf16[32,128,256]{2,0,1:T(8,128)(2,1)S(1)}, u32[]{:S(2)}, u32[]{:S(2)}) async-start(bf16[32,128,256]{2,0,1:T(8,128)(2,1)} %copy.80), calls=%async_computation.3 | async-start | bytes 4194304 | tf_op jit(solution)/shard_map/all_to_all | solution.py:37
  340.6 24.7 %all-to-all-done.3 = bf16[32,128,256]{2,0,1:T(8,128)(2,1)S(1)} async-done(((bf16[32,128,256]{2,0,1:T(8,128)(2,1)}), bf16[32,128,256]{2,0,1:T(8,128)(2,1)S(1)}, u32[]{:S(2)}, u32[]{:S(2)}) %all-to-all-start.3) | async-done | bytes 2097184 | tf_op jit(solution)/shard_map/all_to_all | solution.py:37
  366.5 13.2 %fusion = f32[4096,256]{1,0:T(8,128)} fusion(bf16[4096,256]{1,0:T(8,128)(2,1)S(1)} %bitcast.86, s32[4096]{0:T(1024)S(1)} %bitcast.107), kind=kOutput, calls=%fused_computation.2 | convolution fusion | flops 8606711808 | bytes 6307840 | tf_op jit(solution)/shard_map/dot_general | solution.py:33
  (117 shorter events, 36.7 us)
Async XLA Ops:
  7.2 47.5 %copy-start = (bf16[4096,256]{1,0:T(8,128)(2,1)S(1)}, bf16[4096,256]{1,0:T(8,128)(2,1)}, u32[]{:S(2)}) copy-start(bf16[4096,256]{1,0:T(8,128)(2,1)} %param.12) | copy-start | bytes 6291460
  7.2 3.6 copy-start.11
  7.2 3.6 copy-start.7
  7.2 4.3 %copy-start.9 = (s32[1,2048]{1,0:T(1,128)S(1)}, s32[1,2048]{1,0:T(1,128)}, u32[]{:S(2)}) copy-start(s32[1,2048]{1,0:T(1,128)} %param.16) | copy-start | bytes 24580
  7.2 4.4 %copy-start.10 = (s32[2048]{0:T(1024)S(1)}, s32[2048]{0:T(1024)}, u32[]{:S(2)}) copy-start(s32[2048]{0:T(1024)} %param.17) | copy-start | bytes 24580
  7.2 4.5 %copy-start.8 = (s32[2048]{0:T(1024)S(1)}, s32[2048]{0:T(1024)}, u32[]{:S(2)}) copy-start(s32[2048]{0:T(1024)} %param.15) | copy-start | bytes 24580
  7.2 4.5 %copy-start.12 = (s32[128]{0:T(128)S(1)}, s32[128]{0:T(128)}, u32[]{:S(2)}) copy-start(s32[128]{0:T(128)} %param.20) | copy-start | bytes 1540
  12.1 41.5 %copy-start.6 = (bf16[256,256]{1,0:T(8,128)(2,1)S(1)}, bf16[256,256]{1,0:T(8,128)(2,1)}, u32[]{:S(2)}) copy-start(bf16[256,256]{1,0:T(8,128)(2,1)} %param.22) | copy-start | bytes 393220
  14.3 21.2 %all-to-all-start = ((s32[34,128,1]{0,2,1:T(1,128)}), s32[34,128,1]{0,2,1:T(1,128)S(1)}, u32[]{:S(2)}, u32[]{:S(2)}) async-start(s32[34,128,1]{0,2,1:T(1,128)} %copy.72), calls=%async_computation | async-start | bytes 131072 | tf_op jit(solution)/shard_map/all_to_all | solution.py:37
  38.9 14.5 %all-to-all-start.2 = ((bf16[2,128,256]{2,0,1:T(2,128)(2,1)}), bf16[2,128,256]{2,0,1:T(2,128)(2,1)S(1)}, u32[]{:S(2)}, u32[]{:S(2)}) async-start(bf16[2,128,256]{2,0,1:T(2,128)(2,1)} %copy.77), calls=%async_computation.2 | async-start | bytes 262144 | tf_op jit(solution)/shard_map/all_to_all | solution.py:37
  43.2 88.7 %all-gather.2.cloned.1.call-start = ((), (), s32[]{:S(2)}) async-start(), calls=%async_computation.8 | async-start | bytes 8454144 | tf_op jit(solution)/shard_map/all_gather | solution.py:117
  67.0 7.2 %copy-start.13 = (bf16[64]{0:T(256)(128)(2,1)S(1)}, bf16[64]{0:T(256)(128)(2,1)}, u32[]{:S(2)}) copy-start(bf16[64]{0:T(256)(128)(2,1)} %param.18) | copy-start | bytes 388
  69.5 36.2 %all-to-all-start.1 = ((bf16[32,128,256]{2,0,1:T(8,128)(2,1)}), bf16[32,128,256]{2,0,1:T(8,128)(2,1)S(1)}, u32[]{:S(2)}, u32[]{:S(2)}) async-start(bf16[32,128,256]{2,0,1:T(8,128)(2,1)} %copy.74), calls=%async_computation.1 | async-start | bytes 4194304 | tf_op jit(solution)/shard_map/all_to_all | solution.py:37
  75.6 31.9 %copy-start.4 = (bf16[256,256]{1,0:T(8,128)(2,1)S(1)}, bf16[256,256]{1,0:T(8,128)(2,1)}, u32[]{:S(2)}) copy-start(bf16[256,256]{1,0:T(8,128)(2,1)} %param.21) | copy-start | bytes 393220
  138.2 3.4 copy-start.3
  169.0 107.0 %copy-start.5 = (bf16[128,256]{1,0:T(8,128)(2,1)S(1)}, bf16[128,256]{1,0:T(8,128)(2,1)}, u32[]{:S(2)}) copy-start(bf16[128,256]{1,0:T(8,128)(2,1)} %multiply_convert_fusion) | copy-start | bytes 196612
  169.0 107.0 %all-to-all-start.4 = ((bf16[128,128,256]{2,1,0:T(8,128)(2,1)}), bf16[128,128,256]{2,1,0:T(8,128)(2,1)}, u32[]{:S(2)}, u32[]{:S(2)}) async-start(bf16[128,128,256]{2,1,0:T(8,128)(2,1)} %stack.11), calls=%async_computation.4 | async-start | bytes 16777216 | tf_op jit(solution)/shard_map/all_to_all | solution.py:127
  288.3 23.9 %all-to-all-start.6 = ((bf16[6,128,256]{2,0,1:T(8,128)(2,1)}), bf16[6,128,256]{2,0,1:T(8,128)(2,1)S(1)}, u32[]{:S(2)}, u32[]{:S(2)}) async-start(bf16[6,128,256]{2,0,1:T(8,128)(2,1)} %pad_maximum_fusion.1), calls=%async_computation.6 | async-start | bytes 1048576 | tf_op jit(solution)/shard_map/all_to_all | solution.py:37
  300.2 2.0 copy-start.2
  313.5 18.2 %all-to-all-start.7 = ((f32[4,128,256]{2,0,1:T(4,128)}), f32[4,128,256]{2,0,1:T(4,128)S(1)}, u32[]{:S(2)}, u32[]{:S(2)}) async-start(f32[4,128,256]{2,0,1:T(4,128)} %broadcast_in_dim.55), calls=%async_computation.7 | async-start | bytes 1048576 | tf_op jit(solution)/shard_map/all_to_all | solution.py:37
  331.7 33.6 %all-to-all-start.3 = ((bf16[32,128,256]{2,0,1:T(8,128)(2,1)}), bf16[32,128,256]{2,0,1:T(8,128)(2,1)S(1)}, u32[]{:S(2)}, u32[]{:S(2)}) async-start(bf16[32,128,256]{2,0,1:T(8,128)(2,1)} %copy.80), calls=%async_computation.3 | async-start | bytes 4194304 | tf_op jit(solution)/shard_map/all_to_all | solution.py:37
  366.5 13.3 %copy-start.1 = (bf16[4096,256]{1,0:T(8,128)(2,1)S(1)}, bf16[4096,256]{1,0:T(8,128)(2,1)}, u32[]{:S(2)}) copy-start(bf16[4096,256]{1,0:T(8,128)(2,1)} %param.12) | copy-start | bytes 6291460
Sparse Core Ops, SparseCore 0:
  54.8 77.1 all-gather.1
